TPU v7x, 256 devices: a whole 4x4x8 slice. The times are simulated.
256 devices in a mesh: tm: 64 (over y, z, core), state: 4 (over x).
Axes of the slice: x: 4, y: 4, z: 8, core: 2. Of those that a mesh axis runs over, the one named last changes fastest.
Arguments:
- dynamics: float32 [512, 512], P('state'), may hold values from -1 to 1
- pattern: int32 [4, 4], replicated, may hold values from 0 to 1
- initial_mean: float32 [4, 512], replicated, may hold values from -6 to 6
- observed: float32 [1024, 4], P('tm'), may hold values from -6 to 6
- obs_index: int32 [1024], P('tm'), may hold values from 0 to 511
- obs_noise: float32 [1024], P('tm'), may hold values from 0.5 to 4
Outputs:
- filtered: float32 [1024, 4, 512], P('tm', 'state')
- smoothed: float32 [1024, 4, 512], P('tm', 'state')
All inputs are finite; a program needn't handle non-finite values.
Results may differ from a plain program's by a relative error of at most 0.0003.
Values sent between devices are 32-bit elements; how exact they have to be, the bound alone decides.
No kernel may reach another device: no remote copies, remote signals or barrier semaphores. Data moves between devices by JAX's collectives and lax.ppermute only.
A program may use at most 256 MiB of HBM per device.

v0:
```python
import jax
import jax.numpy as jnp
from jax import lax
from jax.sharding import PartitionSpec as P

AXES = ("tm", "state")


def product(left, right):
    return jnp.dot(left, right, precision=lax.Precision.HIGHEST, preferred_element_type=jnp.float32)


def transposed(left, right):
    return lax.dot_general(
        left,
        right,
        (((1,), (1,)), ((), ())),
        precision=lax.Precision.HIGHEST,
        preferred_element_type=jnp.float32,
    )


def leading(left, right):
    return lax.dot_general(
        left,
        right,
        (((0,), (0,)), ((), ())),
        precision=lax.Precision.HIGHEST,
        preferred_element_type=jnp.float32,
    )


def shifted(block, distance, total):
    route = [(i, i + distance) for i in range(total) if 0 <= i + distance < total]
    return lax.ppermute(block, AXES, route)


def per_device(dynamics, pattern, initial_mean, observed, obs_index, obs_noise):
    state_width = dynamics.shape[1]
    blocks = pattern.shape[0]
    block_span = state_width // blocks
    seq_total = initial_mean.shape[0]
    members = lax.axis_size("state")
    segments = lax.axis_size("tm") * members
    member = lax.axis_index("state")
    segment = lax.axis_index(AXES)
    span = observed.shape[0] // members
    steps_total = span * segments
    present = jnp.maximum(pattern, jnp.eye(blocks, dtype=jnp.int32))
    block_mask = jnp.repeat(jnp.repeat(present, block_span, 0), block_span, 1).astype(jnp.float32)
    transition = lax.all_gather(dynamics, "state", axis=0, tiled=True) * block_mask
    first = member * span
    obs_here = lax.dynamic_slice_in_dim(observed, first, span, 0)
    index_here = lax.dynamic_slice_in_dim(obs_index, first, span, 0)
    noise_here = lax.dynamic_slice_in_dim(obs_noise, first, span, 0)
    gains = 1.0 / (1.0 + noise_here)
    state_index = jnp.arange(state_width, dtype=jnp.int32)
    hits = (state_index[None, :] == index_here[:, None]).astype(jnp.float32)
    scales = 1.0 - gains[:, None] * hits
    global_step = segment * span + jnp.arange(span, dtype=jnp.int32)
    keeps = jnp.where(global_step == steps_total - 1, 0.0, 1.0).astype(jnp.float32)
    pushes = [(gains[j] * obs_here[j])[:, None] * hits[j][None, :] for j in range(span)]
    filt_a = transition * scales[0][:, None]
    filt_b = pushes[0]
    for j in range(1, span):
        filt_a = product(transition, filt_a) * scales[j][:, None]
        filt_b = transposed(filt_b, transition) * scales[j][None, :] + pushes[j]
    last = span - 1
    smooth_q = keeps[last] * (transition.T * scales[last][:, None])
    for j in range(last - 1, -1, -1):
        smooth_q = keeps[j] * (leading(transition, smooth_q) * scales[j][:, None])
    levels = 0
    while 2 ** (levels + 1) < segments:
        levels += 1
    stored_q = []
    for level in range(levels):
        distance = 2**level
        arrived_a, arrived_b = shifted((filt_a, filt_b), distance, segments)
        arrived_q = shifted(smooth_q, -distance, segments)
        usable = segment >= distance
        new_a = product(filt_a, arrived_a)
        new_b = transposed(arrived_b, filt_a) + filt_b
        filt_a = jnp.where(usable, new_a, filt_a)
        filt_b = jnp.where(usable, new_b, filt_b)
        stored_q.append(smooth_q)
        smooth_q = jnp.where(segment + distance < segments, product(smooth_q, arrived_q), smooth_q)
    stored_q.append(smooth_q)
    top = 2**levels
    prefix = transposed(initial_mean, filt_a) + filt_b
    if top < segments:
        arrived = shifted(prefix, top, segments)
        prefix = jnp.where(segment >= top, transposed(arrived, filt_a) + filt_b, prefix)
    entry = jnp.where(segment == 0, initial_mean, shifted(prefix, 1, segments))
    filtered = []
    current = entry
    for j in range(span):
        current = transposed(current, transition) * scales[j][None, :] + pushes[j]
        filtered.append(current)
    filtered = jnp.stack(filtered)
    mapped = product(
        transposed(filtered.reshape(span * seq_total, state_width), transition), transition
    ).reshape(span, seq_total, state_width)
    gaps = filtered - keeps[:, None, None] * mapped * scales[:, None, :]
    offsets = jnp.zeros((seq_total, state_width), jnp.float32)
    for j in range(last, -1, -1):
        offsets = keeps[j] * product(offsets, transition) * scales[j][None, :] + gaps[j]
    for level in range(levels):
        distance = 2**level
        arrived = shifted(offsets, -distance, segments)
        offsets = jnp.where(
            segment + distance < segments, transposed(arrived, stored_q[level]) + offsets, offsets
        )
    if top < segments:
        arrived = shifted(offsets, -top, segments)
        offsets = jnp.where(
            segment + top < segments, transposed(arrived, stored_q[levels]) + offsets, offsets
        )
    current = shifted(offsets, -1, segments)
    smoothed = [None] * span
    for j in range(last, -1, -1):
        current = keeps[j] * product(current, transition) * scales[j][None, :] + gaps[j]
        smoothed[j] = current
    smoothed = jnp.stack(smoothed)
    both = jnp.stack([filtered, smoothed])
    both = lax.all_to_all(both, "state", split_axis=2, concat_axis=1, tiled=True)
    return (both[0], both[1])


def solution(mesh):
    return jax.shard_map(
        per_device,
        mesh=mesh,
        in_specs=(P("state", None), P(), P(), P("tm", None), P("tm"), P("tm")),
        out_specs=(P("tm", "state", None), P("tm", "state", None)),
        check_vma=False,
    )
```

profile of v0, /device:TPU:232, one launch (start us, length us, event | category | flops | bytes accessed | tf_op | source)
XLA Modules:
  0.0 522.6 jit_solution(9289157682158466495)
XLA Ops:
  9.4 27.4 %all-gather.2.cloned.1.call-done = f32[512,512]{1,0:T(8,128)} async-done(((f32[128,512]{1,0:T(8,128)}), f32[512,512]{1,0:T(8,128)}) %all-gather.2.cloned.1.call-update) | async-done | bytes 1048592 | tf_op jit(solution)/shard_map/all_gather | solution.py:51
  46.2 20.8 %collective-permute-done = f32[512,512]{1,0:T(8,128)} collective-permute-done((f32[512,512]{1,0:T(8,128)S(1)}, f32[512,512]{1,0:T(8,128)}, u32[]{:S(2)}, u32[]{:S(2)}) %collective-permute-start) | collective-permute-done | bytes 1048608 | tf_op jit(solution)/shard_map/ppermute | solution.py:35
  70.1 6.3 %collective-permute-start.1 = (f32[512,512]{1,0:T(8,128)S(1)}, f32[512,512]{1,0:T(8,128)}, u32[]{:S(2)}, u32[]{:S(2)}) collective-permute-start(f32[512,512]{1,0:T(8,128)S(1)} %convolution_select_fusion.13), channel_id=1, source_target_pairs={{0,2},{1,3},{2,4},{3,5},{4,6},{5,7},{6,8},{7,9},{8,10},{9,11},{10,... | collective-permute-start | bytes 3145736 | tf_op jit(solution)/shard_map/ppermute | solution.py:35
  77.1 22.1 %collective-permute-done.1 = f32[512,512]{1,0:T(8,128)} collective-permute-done((f32[512,512]{1,0:T(8,128)S(1)}, f32[512,512]{1,0:T(8,128)}, u32[]{:S(2)}, u32[]{:S(2)}) %collective-permute-start.1) | collective-permute-done | bytes 1048608 | tf_op jit(solution)/shard_map/ppermute | solution.py:35
  105.0 4.9 fusion.7
  121.8 4.9 collective-permute-start.3
  129.5 13.0 %collective-permute-done.18 = f32[512,512]{1,0:T(8,128)} collective-permute-done((f32[512,512]{1,0:T(8,128)S(1)}, f32[512,512]{1,0:T(8,128)}, u32[]{:S(2)}, u32[]{:S(2)}) %collective-permute-start.18) | collective-permute-done | bytes 1048608 | tf_op jit(solution)/shard_map/ppermute | solution.py:35
  145.5 6.5 %collective-permute-start.20 = (f32[512,512]{1,0:T(8,128)S(1)}, f32[512,512]{1,0:T(8,128)S(1)}, u32[]{:S(2)}, u32[]{:S(2)}) collective-permute-start(f32[512,512]{1,0:T(8,128)S(1)} %convolution_select_fusion.6), channel_id=1, source_target_pairs={{2,0},{3,1},{4,2},{5,3},{6,4},{7,5},{8,6},{9,7},{10,8},{11,9},{12,... | collective-permute-start | bytes 3145736 | tf_op jit(solution)/shard_map/ppermute | solution.py:35
  153.0 3.7 convolution_select_fusion.10
  164.1 11.0 %collective-permute-done.20 = f32[512,512]{1,0:T(8,128)S(1)} collective-permute-done((f32[512,512]{1,0:T(8,128)S(1)}, f32[512,512]{1,0:T(8,128)S(1)}, u32[]{:S(2)}, u32[]{:S(2)}) %collective-permute-start.20) | collective-permute-done | bytes 1048608 | tf_op jit(solution)/shard_map/ppermute | solution.py:35
  180.3 21.0 %collective-permute-done.7 = f32[4,512]{1,0:T(4,128)S(1)} collective-permute-done((f32[4,512]{1,0:T(4,128)S(1)}, f32[4,512]{1,0:T(4,128)S(1)}, u32[]{:S(2)}, u32[]{:S(2)}) %collective-permute-start.7) | collective-permute-done | bytes 8224 | tf_op jit(solution)/shard_map/ppermute | solution.py:35
  210.0 9.3 %collective-permute-start.5 = (f32[512,512]{1,0:T(8,128)}, f32[512,512]{1,0:T(8,128)}, u32[]{:S(2)}, u32[]{:S(2)}) collective-permute-start(f32[512,512]{1,0:T(8,128)} %convolution_select_fusion.9), channel_id=1, source_target_pairs={{0,32},{1,33},{2,34},{3,35},{4,36},{5,37},{6,38},{7,39},{8,40},{9,... | collective-permute-start | bytes 3145736 | tf_op jit(solution)/shard_map/ppermute | solution.py:35
  222.3 11.1 %collective-permute-done.9 = f32[4,512]{1,0:T(4,128)S(1)} collective-permute-done((f32[4,512]{1,0:T(4,128)S(1)}, f32[4,512]{1,0:T(4,128)S(1)}, u32[]{:S(2)}, u32[]{:S(2)}) %collective-permute-start.9) | collective-permute-done | bytes 8224 | tf_op jit(solution)/shard_map/ppermute | solution.py:35
  237.7 4.7 convolution_select_fusion.4
  242.4 3.9 collective-permute-start.24
  246.3 14.5 %collective-permute-done.10 = f32[4,512]{1,0:T(4,128)S(1)} collective-permute-done((f32[4,512]{1,0:T(4,128)S(1)}, f32[4,512]{1,0:T(4,128)S(1)}, u32[]{:S(2)}, u32[]{:S(2)}) %collective-permute-start.10) | collective-permute-done | bytes 8224 | tf_op jit(solution)/shard_map/ppermute | solution.py:35
  263.0 18.0 %collective-permute-start.11 = (f32[4,512]{1,0:T(4,128)S(1)}, f32[4,512]{1,0:T(4,128)S(1)}, u32[]{:S(2)}, u32[]{:S(2)}) collective-permute-start(f32[4,512]{1,0:T(4,128)S(1)} %fusion.42), channel_id=1, source_target_pairs={{0,16},{1,17},{2,18},{3,19},{4,20},{5,21},{6,22},{7,23},{8,24},{9,... | collective-permute-start | bytes 24584 | tf_op jit(solution)/shard_map/ppermute | solution.py:35
  281.0 4.7 convolution_select_fusion.8
  291.1 6.9 %collective-permute-done.12 = f32[4,512]{1,0:T(4,128)S(1)} collective-permute-done((f32[4,512]{1,0:T(4,128)S(1)}, f32[4,512]{1,0:T(4,128)S(1)}, u32[]{:S(2)}, u32[]{:S(2)}) %collective-permute-start.12) | collective-permute-done | bytes 8224 | tf_op jit(solution)/shard_map/ppermute | solution.py:35
  302.1 4.7 convolution_select_fusion.3
  306.8 4.8 collective-permute-start.26
  313.9 3.7 convolution_select_fusion.7
  324.4 4.4 collective-permute-start.15
  328.8 30.4 %collective-permute-done.26 = f32[512,512]{1,0:T(8,128)} collective-permute-done((f32[512,512]{1,0:T(8,128)}, f32[512,512]{1,0:T(8,128)}, u32[]{:S(2)}, u32[]{:S(2)}) %collective-permute-start.26) | collective-permute-done | bytes 1048608 | tf_op jit(solution)/shard_map/ppermute | solution.py:35
  359.3 4.7 convolution_select_fusion.2
  378.5 20.1 %collective-permute-done.16 = f32[4,512]{1,0:T(4,128)S(1)} collective-permute-done((f32[4,512]{1,0:T(4,128)S(1)}, f32[4,512]{1,0:T(4,128)S(1)}, u32[]{:S(2)}, u32[]{:S(2)}) %collective-permute-start.16) | collective-permute-done | bytes 8224 | tf_op jit(solution)/shard_map/ppermute | solution.py:35
  399.6 32.2 %collective-permute-start.17 = (f32[4,512]{1,0:T(4,128)S(1)}, f32[4,512]{1,0:T(4,128)S(1)}, u32[]{:S(2)}, u32[]{:S(2)}) collective-permute-start(f32[4,512]{1,0:T(4,128)S(1)} %fusion.24), channel_id=1, source_target_pairs={{2,0},{3,1},{4,2},{5,3},{6,4},{7,5},{8,6},{9,7},{10,8},{11,9},{12,... | collective-permute-start | bytes 24584 | tf_op jit(solution)/shard_map/ppermute | solution.py:35
  445.6 4.6 collective-permute-start.21
  457.4 6.7 %collective-permute-done.23 = f32[4,512]{1,0:T(4,128)S(1)} collective-permute-done((f32[4,512]{1,0:T(4,128)S(1)}, f32[4,512]{1,0:T(4,128)S(1)}, u32[]{:S(2)}, u32[]{:S(2)}) %collective-permute-start.23) | collective-permute-done | bytes 8224 | tf_op jit(solution)/shard_map/ppermute | solution.py:35
  468.3 8.4 %collective-permute-done.25 = f32[4,512]{1,0:T(4,128)S(1)} collective-permute-done((f32[4,512]{1,0:T(4,128)S(1)}, f32[4,512]{1,0:T(4,128)S(1)}, u32[]{:S(2)}, u32[]{:S(2)}) %collective-permute-start.25) | collective-permute-done | bytes 8224 | tf_op jit(solution)/shard_map/ppermute | solution.py:35
  488.6 3.9 collective-permute-done.29
  504.1 9.9 %all_to_all.15 = f32[2,4,4,512]{3,1,0,2:T(4,128)S(1)} all-to-all(f32[2,4,4,512]{3,1,0,2:T(4,128)S(1)} %copy.10), channel_id=1, replica_groups=mesh['tm'=64,'state'=4] {'state'}, dimensions={2} | all-to-all | bytes 131072 | tf_op jit(solution)/shard_map/all_to_all | solution.py:125
  (143 shorter events, 154.1 us)
Async XLA Ops:
  7.2 29.6 %all-gather.2.cloned.1.call-start = ((), (), s32[]{:S(2)}) async-start(), calls=%async_computation.1 | async-start | bytes 1310720 | tf_op jit(solution)/shard_map/all_gather | solution.py:51
  43.9 23.0 %collective-permute-start = (f32[512,512]{1,0:T(8,128)S(1)}, f32[512,512]{1,0:T(8,128)}, u32[]{:S(2)}, u32[]{:S(2)}) collective-permute-start(f32[512,512]{1,0:T(8,128)S(1)} %convolution_multiply_fusion.3), channel_id=1, source_target_pairs={{0,1},{1,2},{2,3},{3,4},{4,5},{5,6},{6,7},{7,8},{8,9},{9,10},{10,1... | collective-permute-start | bytes 3145736 | tf_op jit(solution)/shard_map/ppermute | solution.py:35
  70.1 29.1 %collective-permute-start.1 = (f32[512,512]{1,0:T(8,128)S(1)}, f32[512,512]{1,0:T(8,128)}, u32[]{:S(2)}, u32[]{:S(2)}) collective-permute-start(f32[512,512]{1,0:T(8,128)S(1)} %convolution_select_fusion.13), channel_id=1, source_target_pairs={{0,2},{1,3},{2,4},{3,5},{4,6},{5,7},{6,8},{7,9},{8,10},{9,11},{10,... | collective-permute-start | bytes 3145736 | tf_op jit(solution)/shard_map/ppermute | solution.py:35
  102.3 16.6 %collective-permute-start.2 = (f32[512,512]{1,0:T(8,128)S(1)}, f32[512,512]{1,0:T(8,128)S(1)}, u32[]{:S(2)}, u32[]{:S(2)}) collective-permute-start(f32[512,512]{1,0:T(8,128)S(1)} %convolution_select_fusion.12), channel_id=1, source_target_pairs={{0,4},{1,5},{2,6},{3,7},{4,8},{5,9},{6,10},{7,11},{8,12},{9,13},{1... | collective-permute-start | bytes 3145736 | tf_op jit(solution)/shard_map/ppermute | solution.py:35
  115.0 27.5 %collective-permute-start.18 = (f32[512,512]{1,0:T(8,128)S(1)}, f32[512,512]{1,0:T(8,128)}, u32[]{:S(2)}, u32[]{:S(2)}) collective-permute-start(f32[512,512]{1,0:T(8,128)S(1)} %fusion.5), channel_id=1, source_target_pairs={{1,0},{2,1},{3,2},{4,3},{5,4},{6,5},{7,6},{8,7},{9,8},{10,9},{11,1... | collective-permute-start | bytes 3145736 | tf_op jit(solution)/shard_map/ppermute | solution.py:35
  121.8 31.3 %collective-permute-start.3 = (f32[512,512]{1,0:T(8,128)}, f32[512,512]{1,0:T(8,128)}, u32[]{:S(2)}, u32[]{:S(2)}) collective-permute-start(f32[512,512]{1,0:T(8,128)} %convolution_select_fusion.11), channel_id=1, source_target_pairs={{0,8},{1,9},{2,10},{3,11},{4,12},{5,13},{6,14},{7,15},{8,16},{9,17... | collective-permute-start | bytes 3145736 | tf_op jit(solution)/shard_map/ppermute | solution.py:35
  145.5 29.5 %collective-permute-start.20 = (f32[512,512]{1,0:T(8,128)S(1)}, f32[512,512]{1,0:T(8,128)S(1)}, u32[]{:S(2)}, u32[]{:S(2)}) collective-permute-start(f32[512,512]{1,0:T(8,128)S(1)} %convolution_select_fusion.6), channel_id=1, source_target_pairs={{2,0},{3,1},{4,2},{5,3},{6,4},{7,5},{8,6},{9,7},{10,8},{11,9},{12,... | collective-permute-start | bytes 3145736 | tf_op jit(solution)/shard_map/ppermute | solution.py:35
  156.8 50.4 %collective-permute-start.4 = (f32[512,512]{1,0:T(8,128)S(1)}, f32[512,512]{1,0:T(8,128)S(1)}, u32[]{:S(2)}, u32[]{:S(2)}) collective-permute-start(f32[512,512]{1,0:T(8,128)S(1)} %convolution_select_fusion.10), channel_id=1, source_target_pairs={{0,16},{1,17},{2,18},{3,19},{4,20},{5,21},{6,22},{7,23},{8,24},{9,... | collective-permute-start | bytes 3145736 | tf_op jit(solution)/shard_map/ppermute | solution.py:35
  162.0 39.3 %collective-permute-start.7 = (f32[4,512]{1,0:T(4,128)S(1)}, f32[4,512]{1,0:T(4,128)S(1)}, u32[]{:S(2)}, u32[]{:S(2)}) collective-permute-start(f32[4,512]{1,0:T(4,128)S(1)} %fusion.46), channel_id=1, source_target_pairs={{0,1},{1,2},{2,3},{3,4},{4,5},{5,6},{6,7},{7,8},{8,9},{9,10},{10,1... | collective-permute-start | bytes 24584 | tf_op jit(solution)/shard_map/ppermute | solution.py:35
  177.9 59.8 %collective-permute-start.22 = (f32[512,512]{1,0:T(8,128)}, f32[512,512]{1,0:T(8,128)}, u32[]{:S(2)}, u32[]{:S(2)}) collective-permute-start(f32[512,512]{1,0:T(8,128)} %convolution_select_fusion.5), channel_id=1, source_target_pairs={{4,0},{5,1},{6,2},{7,3},{8,4},{9,5},{10,6},{11,7},{12,8},{13,9},{1... | collective-permute-start | bytes 3145736 | tf_op jit(solution)/shard_map/ppermute | solution.py:35
  202.3 17.1 %collective-permute-start.8 = (f32[4,512]{1,0:T(4,128)S(1)}, f32[4,512]{1,0:T(4,128)S(1)}, u32[]{:S(2)}, u32[]{:S(2)}) collective-permute-start(f32[4,512]{1,0:T(4,128)S(1)} %fusion.45), channel_id=1, source_target_pairs={{0,2},{1,3},{2,4},{3,5},{4,6},{5,7},{6,8},{7,9},{8,10},{9,11},{10,... | collective-permute-start | bytes 24584 | tf_op jit(solution)/shard_map/ppermute | solution.py:35
  210.0 70.9 %collective-permute-start.5 = (f32[512,512]{1,0:T(8,128)}, f32[512,512]{1,0:T(8,128)}, u32[]{:S(2)}, u32[]{:S(2)}) collective-permute-start(f32[512,512]{1,0:T(8,128)} %convolution_select_fusion.9), channel_id=1, source_target_pairs={{0,32},{1,33},{2,34},{3,35},{4,36},{5,37},{6,38},{7,39},{8,40},{9,... | collective-permute-start | bytes 3145736 | tf_op jit(solution)/shard_map/ppermute | solution.py:35
  220.4 13.0 %collective-permute-start.9 = (f32[4,512]{1,0:T(4,128)S(1)}, f32[4,512]{1,0:T(4,128)S(1)}, u32[]{:S(2)}, u32[]{:S(2)}) collective-permute-start(f32[4,512]{1,0:T(4,128)S(1)} %fusion.44), channel_id=1, source_target_pairs={{0,4},{1,5},{2,6},{3,7},{4,8},{5,9},{6,10},{7,11},{8,12},{9,13},{1... | collective-permute-start | bytes 24584 | tf_op jit(solution)/shard_map/ppermute | solution.py:35
  235.6 25.2 %collective-permute-start.10 = (f32[4,512]{1,0:T(4,128)S(1)}, f32[4,512]{1,0:T(4,128)S(1)}, u32[]{:S(2)}, u32[]{:S(2)}) collective-permute-start(f32[4,512]{1,0:T(4,128)S(1)} %fusion.43), channel_id=1, source_target_pairs={{0,8},{1,9},{2,10},{3,11},{4,12},{5,13},{6,14},{7,15},{8,16},{9,17... | collective-permute-start | bytes 24584 | tf_op jit(solution)/shard_map/ppermute | solution.py:35
  242.4 59.8 %collective-permute-start.24 = (f32[512,512]{1,0:T(8,128)}, f32[512,512]{1,0:T(8,128)}, u32[]{:S(2)}, u32[]{:S(2)}) collective-permute-start(f32[512,512]{1,0:T(8,128)} %convolution_select_fusion.4), channel_id=1, source_target_pairs={{8,0},{9,1},{10,2},{11,3},{12,4},{13,5},{14,6},{15,7},{16,8},{17,9... | collective-permute-start | bytes 3145736 | tf_op jit(solution)/shard_map/ppermute | solution.py:35
  263.0 24.6 %collective-permute-start.11 = (f32[4,512]{1,0:T(4,128)S(1)}, f32[4,512]{1,0:T(4,128)S(1)}, u32[]{:S(2)}, u32[]{:S(2)}) collective-permute-start(f32[4,512]{1,0:T(4,128)S(1)} %fusion.42), channel_id=1, source_target_pairs={{0,16},{1,17},{2,18},{3,19},{4,20},{5,21},{6,22},{7,23},{8,24},{9,... | collective-permute-start | bytes 24584 | tf_op jit(solution)/shard_map/ppermute | solution.py:35
  285.7 28.2 %collective-permute-start.6 = (f32[512,512]{1,0:T(8,128)}, f32[512,512]{1,0:T(8,128)}, u32[]{:S(2)}, u32[]{:S(2)}) collective-permute-start(f32[512,512]{1,0:T(8,128)} %convolution_select_fusion.8), channel_id=1, source_target_pairs={{0,64},{1,65},{2,66},{3,67},{4,68},{5,69},{6,70},{7,71},{8,72},{9,... | collective-permute-start | bytes 3145736 | tf_op jit(solution)/shard_map/ppermute | solution.py:35
  288.6 9.5 %collective-permute-start.12 = (f32[4,512]{1,0:T(4,128)S(1)}, f32[4,512]{1,0:T(4,128)S(1)}, u32[]{:S(2)}, u32[]{:S(2)}) collective-permute-start(f32[4,512]{1,0:T(4,128)S(1)} %fusion.41), channel_id=1, source_target_pairs={{0,32},{1,33},{2,34},{3,35},{4,36},{5,37},{6,38},{7,39},{8,40},{9,... | collective-permute-start | bytes 24584 | tf_op jit(solution)/shard_map/ppermute | solution.py:35
  300.2 11.5 %collective-permute-start.13 = (f32[4,512]{1,0:T(4,128)S(1)}, f32[4,512]{1,0:T(4,128)S(1)}, u32[]{:S(2)}, u32[]{:S(2)}) collective-permute-start(f32[4,512]{1,0:T(4,128)S(1)} %fusion.40), channel_id=1, source_target_pairs={{0,64},{1,65},{2,66},{3,67},{4,68},{5,69},{6,70},{7,71},{8,72},{9,... | collective-permute-start | bytes 24584 | tf_op jit(solution)/shard_map/ppermute | solution.py:35
  306.8 52.4 %collective-permute-start.26 = (f32[512,512]{1,0:T(8,128)}, f32[512,512]{1,0:T(8,128)}, u32[]{:S(2)}, u32[]{:S(2)}) collective-permute-start(f32[512,512]{1,0:T(8,128)} %convolution_select_fusion.3), channel_id=1, source_target_pairs={{16,0},{17,1},{18,2},{19,3},{20,4},{21,5},{22,6},{23,7},{24,8},{25... | collective-permute-start | bytes 3145736 | tf_op jit(solution)/shard_map/ppermute | solution.py:35
  324.4 41.5 %collective-permute-start.15 = (f32[4,512]{1,0:T(4,128)S(1)}, f32[4,512]{1,0:T(4,128)S(1)}, u32[]{:S(2)}, u32[]{:S(2)}) collective-permute-start(f32[4,512]{1,0:T(4,128)S(1)} %fusion.38), channel_id=1, source_target_pairs={{0,1},{1,2},{2,3},{3,4},{4,5},{5,6},{6,7},{7,8},{8,9},{9,10},{10,1... | collective-permute-start | bytes 24584 | tf_op jit(solution)/shard_map/ppermute | solution.py:35
  364.0 73.5 %collective-permute-start.28 = (f32[512,512]{1,0:T(8,128)}, f32[512,512]{1,0:T(8,128)}, u32[]{:S(2)}, u32[]{:S(2)}) collective-permute-start(f32[512,512]{1,0:T(8,128)} %convolution_select_fusion.2), channel_id=1, source_target_pairs={{32,0},{33,1},{34,2},{35,3},{36,4},{37,5},{38,6},{39,7},{40,8},{41... | collective-permute-start | bytes 3145736 | tf_op jit(solution)/shard_map/ppermute | solution.py:35
  376.6 22.0 %collective-permute-start.16 = (f32[4,512]{1,0:T(4,128)S(1)}, f32[4,512]{1,0:T(4,128)S(1)}, u32[]{:S(2)}, u32[]{:S(2)}) collective-permute-start(f32[4,512]{1,0:T(4,128)S(1)} %fusion.26), channel_id=1, source_target_pairs={{1,0},{2,1},{3,2},{4,3},{5,4},{6,5},{7,6},{8,7},{9,8},{10,9},{11,1... | collective-permute-start | bytes 24584 | tf_op jit(solution)/shard_map/ppermute | solution.py:35
  399.6 33.6 %collective-permute-start.17 = (f32[4,512]{1,0:T(4,128)S(1)}, f32[4,512]{1,0:T(4,128)S(1)}, u32[]{:S(2)}, u32[]{:S(2)}) collective-permute-start(f32[4,512]{1,0:T(4,128)S(1)} %fusion.24), channel_id=1, source_target_pairs={{2,0},{3,1},{4,2},{5,3},{6,4},{7,5},{8,6},{9,7},{10,8},{11,9},{12,... | collective-permute-start | bytes 24584 | tf_op jit(solution)/shard_map/ppermute | solution.py:35
  434.1 9.2 %collective-permute-start.19 = (f32[4,512]{1,0:T(4,128)S(1)}, f32[4,512]{1,0:T(4,128)S(1)}, u32[]{:S(2)}, u32[]{:S(2)}) collective-permute-start(f32[4,512]{1,0:T(4,128)S(1)} %fusion.23), channel_id=1, source_target_pairs={{4,0},{5,1},{6,2},{7,3},{8,4},{9,5},{10,6},{11,7},{12,8},{13,9},{1... | collective-permute-start | bytes 24584 | tf_op jit(solution)/shard_map/ppermute | solution.py:35
  441.2 45.5 %collective-permute-start.30 = (f32[512,512]{1,0:T(8,128)S(1)}, f32[512,512]{1,0:T(8,128)S(1)}, u32[]{:S(2)}, u32[]{:S(2)}) collective-permute-start(f32[512,512]{1,0:T(8,128)S(1)} %convolution_select_fusion.1), channel_id=1, source_target_pairs={{64,0},{65,1},{66,2},{67,3},{68,4},{69,5},{70,6},{71,7},{72,8},{73... | collective-permute-start | bytes 3145736 | tf_op jit(solution)/shard_map/ppermute | solution.py:35
  445.6 7.8 %collective-permute-start.21 = (f32[4,512]{1,0:T(4,128)S(1)}, f32[4,512]{1,0:T(4,128)S(1)}, u32[]{:S(2)}, u32[]{:S(2)}) collective-permute-start(f32[4,512]{1,0:T(4,128)S(1)} %fusion.22), channel_id=1, source_target_pairs={{8,0},{9,1},{10,2},{11,3},{12,4},{13,5},{14,6},{15,7},{16,8},{17,9... | collective-permute-start | bytes 24584 | tf_op jit(solution)/shard_map/ppermute | solution.py:35
  455.5 8.7 %collective-permute-start.23 = (f32[4,512]{1,0:T(4,128)S(1)}, f32[4,512]{1,0:T(4,128)S(1)}, u32[]{:S(2)}, u32[]{:S(2)}) collective-permute-start(f32[4,512]{1,0:T(4,128)S(1)} %fusion.21), channel_id=1, source_target_pairs={{16,0},{17,1},{18,2},{19,3},{20,4},{21,5},{22,6},{23,7},{24,8},{25... | collective-permute-start | bytes 24584 | tf_op jit(solution)/shard_map/ppermute | solution.py:35
  466.4 10.4 %collective-permute-start.25 = (f32[4,512]{1,0:T(4,128)S(1)}, f32[4,512]{1,0:T(4,128)S(1)}, u32[]{:S(2)}, u32[]{:S(2)}) collective-permute-start(f32[4,512]{1,0:T(4,128)S(1)} %fusion.20), channel_id=1, source_target_pairs={{32,0},{33,1},{34,2},{35,3},{36,4},{37,5},{38,6},{39,7},{40,8},{41... | collective-permute-start | bytes 24584 | tf_op jit(solution)/shard_map/ppermute | solution.py:35
  478.9 5.5 %collective-permute-start.27 = (f32[4,512]{1,0:T(4,128)S(1)}, f32[4,512]{1,0:T(4,128)S(1)}, u32[]{:S(2)}, u32[]{:S(2)}) collective-permute-start(f32[4,512]{1,0:T(4,128)S(1)} %fusion.19), channel_id=1, source_target_pairs={{64,0},{65,1},{66,2},{67,3},{68,4},{69,5},{70,6},{71,7},{72,8},{73... | collective-permute-start | bytes 24584 | tf_op jit(solution)/shard_map/ppermute | solution.py:35
  485.4 7.1 %collective-permute-start.29 = (f32[4,512]{1,0:T(4,128)S(1)}, f32[4,512]{1,0:T(4,128)S(1)}, u32[]{:S(2)}, u32[]{:S(2)}) collective-permute-start(f32[4,512]{1,0:T(4,128)S(1)} %fusion.18), channel_id=1, source_target_pairs={{128,0},{129,1},{130,2},{131,3},{132,4},{133,5},{134,6},{135,7},{1... | collective-permute-start | bytes 24584 | tf_op jit(solution)/shard_map/ppermute | solution.py:35
  493.4 5.5 %collective-permute-start.31 = (f32[4,512]{1,0:T(4,128)S(1)}, f32[4,512]{1,0:T(4,128)S(1)}, u32[]{:S(2)}, u32[]{:S(2)}) collective-permute-start(f32[4,512]{1,0:T(4,128)S(1)} %fusion.17), channel_id=1, source_target_pairs={{1,0},{2,1},{3,2},{4,3},{5,4},{6,5},{7,6},{8,7},{9,8},{10,9},{11,1... | collective-permute-start | bytes 24584 | tf_op jit(solution)/shard_map/ppermute | solution.py:35
  (15 other events, 329.0 us)
Sparse Core Ops, SparseCore 0:
  9.8 26.9 all-gather.1
where the time goes:
time: 532 us; the launch traced here: 523 us
  waiting for transfers between devices  234 us (44%)
  starting transfers between devices  143 us (27%)
  matrix products  111 us (21%)
  between operations  15.2 us (3%)
  blocking collectives  9.88 us (2%)
  local copies, waits for them, and re-layouts  6.3 us (1%)
    ppermute x32, waiting for transfers between devices, shifted(): return lax.ppermute(block, AXES, route)  206 us
    ppermute x32, starting transfers between devices, shifted(): return lax.ppermute(block, AXES, route)  143 us
    dot_general x26, matrix products, product(): jnp.dot(left, right, precision=lax.Precision.HIGHEST, preferred_element_t...  66.1 us
    dot_general x25, matrix products, transposed(): lax.dot_general(left, right, (((1,), (1,)), ((), ())), precision=lax.Prec...  35.1 us
    all_gather x1, waiting for transfers between devices, per_device(): lax.all_gather(dynamics, 'state', axis=0, tiled=True) * block_mask  27.4 us
  transfers between devices with their start and end apart: 33, of which 20 were waited for; matrix products, arithmetic and copies ran while one was open for 19% of the time, Pallas kernels for 0%

commit v1 on v0

--- a/solution.py
+++ b/solution.py
@@ -4,6 +4,19 @@
 from jax.sharding import PartitionSpec as P
 
 AXES = ("tm", "state")
+
+
+def gather_around(x, axis, dim):
+    ways = lax.axis_size(axis)
+    up = [(d, (d + 1) % ways) for d in range(ways)]
+    down = [(d, (d - 1) % ways) for d in range(ways)]
+    earlier, later = ([x], [x])
+    for _ in range(ways // 2):
+        earlier.append(lax.ppermute(earlier[-1], axis, up))
+    for _ in range((ways - 1) // 2):
+        later.append(lax.ppermute(later[-1], axis, down))
+    line = jnp.concatenate([*earlier[::-1], *later[1:]], axis=dim)
+    return jnp.roll(line, (lax.axis_index(axis) - ways // 2) * x.shape[dim], axis=dim)
 
 
 def product(left, right):
@@ -48,7 +61,7 @@
     steps_total = span * segments
     present = jnp.maximum(pattern, jnp.eye(blocks, dtype=jnp.int32))
     block_mask = jnp.repeat(jnp.repeat(present, block_span, 0), block_span, 1).astype(jnp.float32)
-    transition = lax.all_gather(dynamics, "state", axis=0, tiled=True) * block_mask
+    transition = gather_around(dynamics, "state", 0) * block_mask
     first = member * span
     obs_here = lax.dynamic_slice_in_dim(observed, first, span, 0)
     index_here = lax.dynamic_slice_in_dim(obs_index, first, span, 0)

time: 532 us -> 501 us (0.942)
  waiting for transfers between devices: 234 us -> 217 us
  between operations: 15.2 us -> 1.88 us
  starting transfers between devices: 143 us -> 135 us
  blocking collectives: 9.88 us -> 16.9 us
    all_gather x1 -> x0, waiting for transfers between devices: 27.4 us -> none  [per_device(): lax.all_gather(dynamics, 'state', axis=0, tiled=True) * block_mask]
    ppermute x0 -> x3, waiting for transfers between devices: none -> 12.1 us  [the longest x2 12.1 us: gather_around(): earlier.append(lax.ppermute(earlier[-1], axis, up))]
    ppermute x32, starting transfers between devices: 143 us -> 131 us  [shifted(): return lax.ppermute(block, AXES, route)]
    all_to_all x1, blocking collectives: 9.88 us -> 16.9 us  [per_device(): lax.all_to_all(both, 'state', split_axis=2, concat_axis=1, tiled=True)]
  transfers between devices with their start and end apart: 33 -> 35, of which waited for: 20 -> 20; matrix products, arithmetic and copies ran while one was open for 19% -> 20% of each run, Pallas kernels for 0% -> 0%
where the time goes in v1:
time: 501 us; the launch traced here: 492 us
  waiting for transfers between devices  217 us (43%)
  starting transfers between devices  135 us (27%)
  matrix products  111 us (22%)
  blocking collectives  16.9 us (3%)
  local copies, waits for them, and re-layouts  6.29 us (1%)
    ppermute x32, waiting for transfers between devices, shifted(): return lax.ppermute(block, AXES, route)  204 us
    ppermute x32, starting transfers between devices, shifted(): return lax.ppermute(block, AXES, route)  131 us
    dot_general x26, matrix products, product(): jnp.dot(left, right, precision=lax.Precision.HIGHEST, preferred_element_t...  65.9 us
    dot_general x25, matrix products, transposed(): lax.dot_general(left, right, (((1,), (1,)), ((), ())), precision=lax.Prec...  35.1 us
    all_to_all x1, blocking collectives, per_device(): lax.all_to_all(both, 'state', split_axis=2, concat_axis=1, tiled=True)  16.9 us
    ppermute x2, waiting for transfers between devices, gather_around(): earlier.append(lax.ppermute(earlier[-1], axis, up))  12.1 us
  transfers between devices with their start and end apart: 35, of which 20 were waited for; matrix products, arithmetic and copies ran while one was open for 20% of the time, Pallas kernels for 0%

profile of v1, /device:TPU:232, one launch (start us, length us, event | category | flops | bytes accessed | tf_op | source)
XLA Modules:
  0.0 492.1 jit_solution(306803109408773723)
XLA Ops:
  5.5 4.7 collective-permute-done
  11.2 7.4 %collective-permute-done.1 = f32[128,512]{1,0:T(8,128)S(1)} collective-permute-done((f32[128,512]{1,0:T(8,128)S(1)}, f32[128,512]{1,0:T(8,128)S(1)}, u32[]{:S(2)}, u32[]{:S(2)}) %collective-permute-start.1) | collective-permute-done | bytes 262176 | tf_op jit(solution)/shard_map/ppermute | solution.py:15
  28.3 21.0 %collective-permute-done.3 = f32[512,512]{1,0:T(8,128)} collective-permute-done((f32[512,512]{1,0:T(8,128)S(1)}, f32[512,512]{1,0:T(8,128)}, u32[]{:S(2)}, u32[]{:S(2)}) %collective-permute-start.3) | collective-permute-done | bytes 1048608 | tf_op jit(solution)/shard_map/ppermute | solution.py:48
  52.3 5.0 %collective-permute-start.4 = (f32[512,512]{1,0:T(8,128)S(1)}, f32[512,512]{1,0:T(8,128)}, u32[]{:S(2)}, u32[]{:S(2)}) collective-permute-start(f32[512,512]{1,0:T(8,128)S(1)} %convolution_select_fusion.13), channel_id=1, source_target_pairs={{0,2},{1,3},{2,4},{3,5},{4,6},{5,7},{6,8},{7,9},{8,10},{9,11},{10,... | collective-permute-start | bytes 3145736 | tf_op jit(solution)/shard_map/ppermute | solution.py:48
  58.0 22.3 %collective-permute-done.4 = f32[512,512]{1,0:T(8,128)} collective-permute-done((f32[512,512]{1,0:T(8,128)S(1)}, f32[512,512]{1,0:T(8,128)}, u32[]{:S(2)}, u32[]{:S(2)}) %collective-permute-start.4) | collective-permute-done | bytes 1048608 | tf_op jit(solution)/shard_map/ppermute | solution.py:48
  87.0 4.8 fusion.7
  103.0 5.4 %collective-permute-start.6 = (f32[512,512]{1,0:T(8,128)}, f32[512,512]{1,0:T(8,128)}, u32[]{:S(2)}, u32[]{:S(2)}) collective-permute-start(f32[512,512]{1,0:T(8,128)} %convolution_select_fusion.11), channel_id=1, source_target_pairs={{0,8},{1,9},{2,10},{3,11},{4,12},{5,13},{6,14},{7,15},{8,16},{9,17... | collective-permute-start | bytes 3145736 | tf_op jit(solution)/shard_map/ppermute | solution.py:48
  111.3 12.7 %collective-permute-done.21 = f32[512,512]{1,0:T(8,128)} collective-permute-done((f32[512,512]{1,0:T(8,128)S(1)}, f32[512,512]{1,0:T(8,128)}, u32[]{:S(2)}, u32[]{:S(2)}) %collective-permute-start.21) | collective-permute-done | bytes 1048608 | tf_op jit(solution)/shard_map/ppermute | solution.py:48
  127.1 5.6 %collective-permute-start.23 = (f32[512,512]{1,0:T(8,128)S(1)}, f32[512,512]{1,0:T(8,128)S(1)}, u32[]{:S(2)}, u32[]{:S(2)}) collective-permute-start(f32[512,512]{1,0:T(8,128)S(1)} %convolution_select_fusion.6), channel_id=1, source_target_pairs={{2,0},{3,1},{4,2},{5,3},{6,4},{7,5},{8,6},{9,7},{10,8},{11,9},{12,... | collective-permute-start | bytes 3145736 | tf_op jit(solution)/shard_map/ppermute | solution.py:48
  143.3 11.6 %collective-permute-done.23 = f32[512,512]{1,0:T(8,128)S(1)} collective-permute-done((f32[512,512]{1,0:T(8,128)S(1)}, f32[512,512]{1,0:T(8,128)S(1)}, u32[]{:S(2)}, u32[]{:S(2)}) %collective-permute-start.23) | collective-permute-done | bytes 1048608 | tf_op jit(solution)/shard_map/ppermute | solution.py:48
  161.2 25.2 %collective-permute-done.10 = f32[4,512]{1,0:T(4,128)S(1)} collective-permute-done((f32[4,512]{1,0:T(4,128)S(1)}, f32[4,512]{1,0:T(4,128)S(1)}, u32[]{:S(2)}, u32[]{:S(2)}) %collective-permute-start.10) | collective-permute-done | bytes 8224 | tf_op jit(solution)/shard_map/ppermute | solution.py:48
  192.2 6.7 %collective-permute-start.8 = (f32[512,512]{1,0:T(8,128)}, f32[512,512]{1,0:T(8,128)}, u32[]{:S(2)}, u32[]{:S(2)}) collective-permute-start(f32[512,512]{1,0:T(8,128)} %convolution_select_fusion.9), channel_id=1, source_target_pairs={{0,32},{1,33},{2,34},{3,35},{4,36},{5,37},{6,38},{7,39},{8,40},{9,... | collective-permute-start | bytes 3145736 | tf_op jit(solution)/shard_map/ppermute | solution.py:48
  202.0 20.4 %collective-permute-done.12 = f32[4,512]{1,0:T(4,128)S(1)} collective-permute-done((f32[4,512]{1,0:T(4,128)S(1)}, f32[4,512]{1,0:T(4,128)S(1)}, u32[]{:S(2)}, u32[]{:S(2)}) %collective-permute-start.12) | collective-permute-done | bytes 8224 | tf_op jit(solution)/shard_map/ppermute | solution.py:48
  226.5 4.7 convolution_select_fusion.4
  231.2 4.0 collective-permute-start.27
  235.3 7.9 %collective-permute-done.13 = f32[4,512]{1,0:T(4,128)S(1)} collective-permute-done((f32[4,512]{1,0:T(4,128)S(1)}, f32[4,512]{1,0:T(4,128)S(1)}, u32[]{:S(2)}, u32[]{:S(2)}) %collective-permute-start.13) | collective-permute-done | bytes 8224 | tf_op jit(solution)/shard_map/ppermute | solution.py:48
  245.4 17.1 %collective-permute-start.14 = (f32[4,512]{1,0:T(4,128)S(1)}, f32[4,512]{1,0:T(4,128)S(1)}, u32[]{:S(2)}, u32[]{:S(2)}) collective-permute-start(f32[4,512]{1,0:T(4,128)S(1)} %fusion.42), channel_id=1, source_target_pairs={{0,16},{1,17},{2,18},{3,19},{4,20},{5,21},{6,22},{7,23},{8,24},{9,... | collective-permute-start | bytes 24584 | tf_op jit(solution)/shard_map/ppermute | solution.py:48
  262.5 4.7 convolution_select_fusion.8
  270.1 4.0 collective-permute-start.15
  274.1 5.4 %collective-permute-done.15 = f32[4,512]{1,0:T(4,128)S(1)} collective-permute-done((f32[4,512]{1,0:T(4,128)S(1)}, f32[4,512]{1,0:T(4,128)S(1)}, u32[]{:S(2)}, u32[]{:S(2)}) %collective-permute-start.15) | collective-permute-done | bytes 8224 | tf_op jit(solution)/shard_map/ppermute | solution.py:48
  283.6 4.7 convolution_select_fusion.3
  288.3 5.1 %collective-permute-start.29 = (f32[512,512]{1,0:T(8,128)}, f32[512,512]{1,0:T(8,128)}, u32[]{:S(2)}, u32[]{:S(2)}) collective-permute-start(f32[512,512]{1,0:T(8,128)} %convolution_select_fusion.3), channel_id=1, source_target_pairs={{16,0},{17,1},{18,2},{19,3},{20,4},{21,5},{22,6},{23,7},{24,8},{25... | collective-permute-start | bytes 3145736 | tf_op jit(solution)/shard_map/ppermute | solution.py:48
  308.1 30.7 %collective-permute-done.29 = f32[512,512]{1,0:T(8,128)} collective-permute-done((f32[512,512]{1,0:T(8,128)}, f32[512,512]{1,0:T(8,128)}, u32[]{:S(2)}, u32[]{:S(2)}) %collective-permute-start.29) | collective-permute-done | bytes 1048608 | tf_op jit(solution)/shard_map/ppermute | solution.py:48
  338.8 4.7 convolution_select_fusion.2
  358.4 20.2 %collective-permute-done.19 = f32[4,512]{1,0:T(4,128)S(1)} collective-permute-done((f32[4,512]{1,0:T(4,128)S(1)}, f32[4,512]{1,0:T(4,128)S(1)}, u32[]{:S(2)}, u32[]{:S(2)}) %collective-permute-start.19) | collective-permute-done | bytes 8224 | tf_op jit(solution)/shard_map/ppermute | solution.py:48
  379.6 9.6 %collective-permute-start.20 = (f32[4,512]{1,0:T(4,128)S(1)}, f32[4,512]{1,0:T(4,128)S(1)}, u32[]{:S(2)}, u32[]{:S(2)}) collective-permute-start(f32[4,512]{1,0:T(4,128)S(1)} %fusion.24), channel_id=1, source_target_pairs={{2,0},{3,1},{4,2},{5,3},{6,4},{7,5},{8,6},{9,7},{10,8},{11,9},{12,... | collective-permute-start | bytes 24584 | tf_op jit(solution)/shard_map/ppermute | solution.py:48
  391.5 4.3 collective-permute-start.22
  403.7 17.8 %collective-permute-start.24 = (f32[4,512]{1,0:T(4,128)S(1)}, f32[4,512]{1,0:T(4,128)S(1)}, u32[]{:S(2)}, u32[]{:S(2)}) collective-permute-start(f32[4,512]{1,0:T(4,128)S(1)} %fusion.22), channel_id=1, source_target_pairs={{8,0},{9,1},{10,2},{11,3},{12,4},{13,5},{14,6},{15,7},{16,8},{17,9... | collective-permute-start | bytes 24584 | tf_op jit(solution)/shard_map/ppermute | solution.py:48
  428.6 4.9 collective-permute-done.26
  438.8 7.3 %collective-permute-done.28 = f32[4,512]{1,0:T(4,128)S(1)} collective-permute-done((f32[4,512]{1,0:T(4,128)S(1)}, f32[4,512]{1,0:T(4,128)S(1)}, u32[]{:S(2)}, u32[]{:S(2)}) %collective-permute-start.28) | collective-permute-done | bytes 8224 | tf_op jit(solution)/shard_map/ppermute | solution.py:48
  457.9 3.9 collective-permute-done.32
  473.4 16.9 %all_to_all.15 = f32[2,4,4,512]{3,1,0,2:T(4,128)S(1)} all-to-all(f32[2,4,4,512]{3,1,0,2:T(4,128)S(1)} %copy.10), channel_id=1, replica_groups=mesh['tm'=64,'state'=4] {'state'}, dimensions={2} | all-to-all | bytes 131072 | tf_op jit(solution)/shard_map/all_to_all | solution.py:138
  (148 shorter events, 159.5 us)
Async XLA Ops:
  0.7 9.5 %collective-permute-start = (f32[128,512]{1,0:T(8,128)}, f32[128,512]{1,0:T(8,128)S(1)}, u32[]{:S(2)}, u32[]{:S(2)}) collective-permute-start(f32[128,512]{1,0:T(8,128)} %param.6), channel_id=1, source_target_pairs={{0,1},{1,2},{2,3},{3,0},{4,5},{5,6},{6,7},{7,4},{8,9},{9,10},{10,1... | collective-permute-start | bytes 786440 | tf_op jit(solution)/shard_map/ppermute | solution.py:15
  2.2 17.4 %collective-permute-start.2 = (f32[128,512]{1,0:T(8,128)}, f32[128,512]{1,0:T(8,128)S(1)}, u32[]{:S(2)}, u32[]{:S(2)}) collective-permute-start(f32[128,512]{1,0:T(8,128)} %param.6), channel_id=1, source_target_pairs={{0,3},{1,0},{2,1},{3,2},{4,7},{5,4},{6,5},{7,6},{8,11},{9,8},{10,9... | collective-permute-start | bytes 786440 | tf_op jit(solution)/shard_map/ppermute | solution.py:17
  10.2 8.4 %collective-permute-start.1 = (f32[128,512]{1,0:T(8,128)S(1)}, f32[128,512]{1,0:T(8,128)S(1)}, u32[]{:S(2)}, u32[]{:S(2)}) collective-permute-start(f32[128,512]{1,0:T(8,128)S(1)} %collective-permute-done), channel_id=1, source_target_pairs={{0,1},{1,2},{2,3},{3,0},{4,5},{5,6},{6,7},{7,4},{8,9},{9,10},{10,1... | collective-permute-start | bytes 786440 | tf_op jit(solution)/shard_map/ppermute | solution.py:15
  26.3 22.9 %collective-permute-start.3 = (f32[512,512]{1,0:T(8,128)S(1)}, f32[512,512]{1,0:T(8,128)}, u32[]{:S(2)}, u32[]{:S(2)}) collective-permute-start(f32[512,512]{1,0:T(8,128)S(1)} %convolution_multiply_fusion.3), channel_id=1, source_target_pairs={{0,1},{1,2},{2,3},{3,4},{4,5},{5,6},{6,7},{7,8},{8,9},{9,10},{10,1... | collective-permute-start | bytes 3145736 | tf_op jit(solution)/shard_map/ppermute | solution.py:48
  52.3 28.0 %collective-permute-start.4 = (f32[512,512]{1,0:T(8,128)S(1)}, f32[512,512]{1,0:T(8,128)}, u32[]{:S(2)}, u32[]{:S(2)}) collective-permute-start(f32[512,512]{1,0:T(8,128)S(1)} %convolution_select_fusion.13), channel_id=1, source_target_pairs={{0,2},{1,3},{2,4},{3,5},{4,6},{5,7},{6,8},{7,9},{8,10},{9,11},{10,... | collective-permute-start | bytes 3145736 | tf_op jit(solution)/shard_map/ppermute | solution.py:48
  83.4 16.7 %collective-permute-start.5 = (f32[512,512]{1,0:T(8,128)S(1)}, f32[512,512]{1,0:T(8,128)S(1)}, u32[]{:S(2)}, u32[]{:S(2)}) collective-permute-start(f32[512,512]{1,0:T(8,128)S(1)} %convolution_select_fusion.12), channel_id=1, source_target_pairs={{0,4},{1,5},{2,6},{3,7},{4,8},{5,9},{6,10},{7,11},{8,12},{9,13},{1... | collective-permute-start | bytes 3145736 | tf_op jit(solution)/shard_map/ppermute | solution.py:48
  96.9 27.1 %collective-permute-start.21 = (f32[512,512]{1,0:T(8,128)S(1)}, f32[512,512]{1,0:T(8,128)}, u32[]{:S(2)}, u32[]{:S(2)}) collective-permute-start(f32[512,512]{1,0:T(8,128)S(1)} %fusion.5), channel_id=1, source_target_pairs={{1,0},{2,1},{3,2},{4,3},{5,4},{6,5},{7,6},{8,7},{9,8},{10,9},{11,1... | collective-permute-start | bytes 3145736 | tf_op jit(solution)/shard_map/ppermute | solution.py:48
  103.0 30.7 %collective-permute-start.6 = (f32[512,512]{1,0:T(8,128)}, f32[512,512]{1,0:T(8,128)}, u32[]{:S(2)}, u32[]{:S(2)}) collective-permute-start(f32[512,512]{1,0:T(8,128)} %convolution_select_fusion.11), channel_id=1, source_target_pairs={{0,8},{1,9},{2,10},{3,11},{4,12},{5,13},{6,14},{7,15},{8,16},{9,17... | collective-permute-start | bytes 3145736 | tf_op jit(solution)/shard_map/ppermute | solution.py:48
  127.1 27.7 %collective-permute-start.23 = (f32[512,512]{1,0:T(8,128)S(1)}, f32[512,512]{1,0:T(8,128)S(1)}, u32[]{:S(2)}, u32[]{:S(2)}) collective-permute-start(f32[512,512]{1,0:T(8,128)S(1)} %convolution_select_fusion.6), channel_id=1, source_target_pairs={{2,0},{3,1},{4,2},{5,3},{6,4},{7,5},{8,6},{9,7},{10,8},{11,9},{12,... | collective-permute-start | bytes 3145736 | tf_op jit(solution)/shard_map/ppermute | solution.py:48
  137.4 51.9 %collective-permute-start.7 = (f32[512,512]{1,0:T(8,128)S(1)}, f32[512,512]{1,0:T(8,128)S(1)}, u32[]{:S(2)}, u32[]{:S(2)}) collective-permute-start(f32[512,512]{1,0:T(8,128)S(1)} %convolution_select_fusion.10), channel_id=1, source_target_pairs={{0,16},{1,17},{2,18},{3,19},{4,20},{5,21},{6,22},{7,23},{8,24},{9,... | collective-permute-start | bytes 3145736 | tf_op jit(solution)/shard_map/ppermute | solution.py:48
  141.3 45.1 %collective-permute-start.10 = (f32[4,512]{1,0:T(4,128)S(1)}, f32[4,512]{1,0:T(4,128)S(1)}, u32[]{:S(2)}, u32[]{:S(2)}) collective-permute-start(f32[4,512]{1,0:T(4,128)S(1)} %fusion.46), channel_id=1, source_target_pairs={{0,1},{1,2},{2,3},{3,4},{4,5},{5,6},{6,7},{7,8},{8,9},{9,10},{10,1... | collective-permute-start | bytes 24584 | tf_op jit(solution)/shard_map/ppermute | solution.py:48
  157.7 68.8 %collective-permute-start.25 = (f32[512,512]{1,0:T(8,128)}, f32[512,512]{1,0:T(8,128)}, u32[]{:S(2)}, u32[]{:S(2)}) collective-permute-start(f32[512,512]{1,0:T(8,128)} %convolution_select_fusion.5), channel_id=1, source_target_pairs={{4,0},{5,1},{6,2},{7,3},{8,4},{9,5},{10,6},{11,7},{12,8},{13,9},{1... | collective-permute-start | bytes 3145736 | tf_op jit(solution)/shard_map/ppermute | solution.py:48
  187.4 11.6 %collective-permute-start.11 = (f32[4,512]{1,0:T(4,128)S(1)}, f32[4,512]{1,0:T(4,128)S(1)}, u32[]{:S(2)}, u32[]{:S(2)}) collective-permute-start(f32[4,512]{1,0:T(4,128)S(1)} %fusion.45), channel_id=1, source_target_pairs={{0,2},{1,3},{2,4},{3,5},{4,6},{5,7},{6,8},{7,9},{8,10},{9,11},{10,... | collective-permute-start | bytes 24584 | tf_op jit(solution)/shard_map/ppermute | solution.py:48
  192.2 70.3 %collective-permute-start.8 = (f32[512,512]{1,0:T(8,128)}, f32[512,512]{1,0:T(8,128)}, u32[]{:S(2)}, u32[]{:S(2)}) collective-permute-start(f32[512,512]{1,0:T(8,128)} %convolution_select_fusion.9), channel_id=1, source_target_pairs={{0,32},{1,33},{2,34},{3,35},{4,36},{5,37},{6,38},{7,39},{8,40},{9,... | collective-permute-start | bytes 3145736 | tf_op jit(solution)/shard_map/ppermute | solution.py:48
  199.9 22.5 %collective-permute-start.12 = (f32[4,512]{1,0:T(4,128)S(1)}, f32[4,512]{1,0:T(4,128)S(1)}, u32[]{:S(2)}, u32[]{:S(2)}) collective-permute-start(f32[4,512]{1,0:T(4,128)S(1)} %fusion.44), channel_id=1, source_target_pairs={{0,4},{1,5},{2,6},{3,7},{4,8},{5,9},{6,10},{7,11},{8,12},{9,13},{1... | collective-permute-start | bytes 24584 | tf_op jit(solution)/shard_map/ppermute | solution.py:48
  224.6 18.6 %collective-permute-start.13 = (f32[4,512]{1,0:T(4,128)S(1)}, f32[4,512]{1,0:T(4,128)S(1)}, u32[]{:S(2)}, u32[]{:S(2)}) collective-permute-start(f32[4,512]{1,0:T(4,128)S(1)} %fusion.43), channel_id=1, source_target_pairs={{0,8},{1,9},{2,10},{3,11},{4,12},{5,13},{6,14},{7,15},{8,16},{9,17... | collective-permute-start | bytes 24584 | tf_op jit(solution)/shard_map/ppermute | solution.py:48
  231.2 52.4 %collective-permute-start.27 = (f32[512,512]{1,0:T(8,128)}, f32[512,512]{1,0:T(8,128)}, u32[]{:S(2)}, u32[]{:S(2)}) collective-permute-start(f32[512,512]{1,0:T(8,128)} %convolution_select_fusion.4), channel_id=1, source_target_pairs={{8,0},{9,1},{10,2},{11,3},{12,4},{13,5},{14,6},{15,7},{16,8},{17,9... | collective-permute-start | bytes 3145736 | tf_op jit(solution)/shard_map/ppermute | solution.py:48
  245.4 23.7 %collective-permute-start.14 = (f32[4,512]{1,0:T(4,128)S(1)}, f32[4,512]{1,0:T(4,128)S(1)}, u32[]{:S(2)}, u32[]{:S(2)}) collective-permute-start(f32[4,512]{1,0:T(4,128)S(1)} %fusion.42), channel_id=1, source_target_pairs={{0,16},{1,17},{2,18},{3,19},{4,20},{5,21},{6,22},{7,23},{8,24},{9,... | collective-permute-start | bytes 24584 | tf_op jit(solution)/shard_map/ppermute | solution.py:48
  267.2 28.5 %collective-permute-start.9 = (f32[512,512]{1,0:T(8,128)}, f32[512,512]{1,0:T(8,128)}, u32[]{:S(2)}, u32[]{:S(2)}) collective-permute-start(f32[512,512]{1,0:T(8,128)} %convolution_select_fusion.8), channel_id=1, source_target_pairs={{0,64},{1,65},{2,66},{3,67},{4,68},{5,69},{6,70},{7,71},{8,72},{9,... | collective-permute-start | bytes 3145736 | tf_op jit(solution)/shard_map/ppermute | solution.py:48
  270.1 9.5 %collective-permute-start.15 = (f32[4,512]{1,0:T(4,128)S(1)}, f32[4,512]{1,0:T(4,128)S(1)}, u32[]{:S(2)}, u32[]{:S(2)}) collective-permute-start(f32[4,512]{1,0:T(4,128)S(1)} %fusion.41), channel_id=1, source_target_pairs={{0,32},{1,33},{2,34},{3,35},{4,36},{5,37},{6,38},{7,39},{8,40},{9,... | collective-permute-start | bytes 24584 | tf_op jit(solution)/shard_map/ppermute | solution.py:48
  281.7 11.7 %collective-permute-start.16 = (f32[4,512]{1,0:T(4,128)S(1)}, f32[4,512]{1,0:T(4,128)S(1)}, u32[]{:S(2)}, u32[]{:S(2)}) collective-permute-start(f32[4,512]{1,0:T(4,128)S(1)} %fusion.40), channel_id=1, source_target_pairs={{0,64},{1,65},{2,66},{3,67},{4,68},{5,69},{6,70},{7,71},{8,72},{9,... | collective-permute-start | bytes 24584 | tf_op jit(solution)/shard_map/ppermute | solution.py:48
  288.3 50.4 %collective-permute-start.29 = (f32[512,512]{1,0:T(8,128)}, f32[512,512]{1,0:T(8,128)}, u32[]{:S(2)}, u32[]{:S(2)}) collective-permute-start(f32[512,512]{1,0:T(8,128)} %convolution_select_fusion.3), channel_id=1, source_target_pairs={{16,0},{17,1},{18,2},{19,3},{20,4},{21,5},{22,6},{23,7},{24,8},{25... | collective-permute-start | bytes 3145736 | tf_op jit(solution)/shard_map/ppermute | solution.py:48
  306.2 39.2 %collective-permute-start.18 = (f32[4,512]{1,0:T(4,128)S(1)}, f32[4,512]{1,0:T(4,128)S(1)}, u32[]{:S(2)}, u32[]{:S(2)}) collective-permute-start(f32[4,512]{1,0:T(4,128)S(1)} %fusion.38), channel_id=1, source_target_pairs={{0,1},{1,2},{2,3},{3,4},{4,5},{5,6},{6,7},{7,8},{8,9},{9,10},{10,1... | collective-permute-start | bytes 24584 | tf_op jit(solution)/shard_map/ppermute | solution.py:48
  343.5 52.3 %collective-permute-start.31 = (f32[512,512]{1,0:T(8,128)}, f32[512,512]{1,0:T(8,128)}, u32[]{:S(2)}, u32[]{:S(2)}) collective-permute-start(f32[512,512]{1,0:T(8,128)} %convolution_select_fusion.2), channel_id=1, source_target_pairs={{32,0},{33,1},{34,2},{35,3},{36,4},{37,5},{38,6},{39,7},{40,8},{41... | collective-permute-start | bytes 3145736 | tf_op jit(solution)/shard_map/ppermute | solution.py:48
  356.0 22.6 %collective-permute-start.19 = (f32[4,512]{1,0:T(4,128)S(1)}, f32[4,512]{1,0:T(4,128)S(1)}, u32[]{:S(2)}, u32[]{:S(2)}) collective-permute-start(f32[4,512]{1,0:T(4,128)S(1)} %fusion.26), channel_id=1, source_target_pairs={{1,0},{2,1},{3,2},{4,3},{5,4},{6,5},{7,6},{8,7},{9,8},{10,9},{11,1... | collective-permute-start | bytes 24584 | tf_op jit(solution)/shard_map/ppermute | solution.py:48
  379.6 11.0 %collective-permute-start.20 = (f32[4,512]{1,0:T(4,128)S(1)}, f32[4,512]{1,0:T(4,128)S(1)}, u32[]{:S(2)}, u32[]{:S(2)}) collective-permute-start(f32[4,512]{1,0:T(4,128)S(1)} %fusion.24), channel_id=1, source_target_pairs={{2,0},{3,1},{4,2},{5,3},{6,4},{7,5},{8,6},{9,7},{10,8},{11,9},{12,... | collective-permute-start | bytes 24584 | tf_op jit(solution)/shard_map/ppermute | solution.py:48
  391.5 10.0 %collective-permute-start.22 = (f32[4,512]{1,0:T(4,128)S(1)}, f32[4,512]{1,0:T(4,128)S(1)}, u32[]{:S(2)}, u32[]{:S(2)}) collective-permute-start(f32[4,512]{1,0:T(4,128)S(1)} %fusion.23), channel_id=1, source_target_pairs={{4,0},{5,1},{6,2},{7,3},{8,4},{9,5},{10,6},{11,7},{12,8},{13,9},{1... | collective-permute-start | bytes 24584 | tf_op jit(solution)/shard_map/ppermute | solution.py:48
  399.5 56.5 %collective-permute-start.33 = (f32[512,512]{1,0:T(8,128)S(1)}, f32[512,512]{1,0:T(8,128)S(1)}, u32[]{:S(2)}, u32[]{:S(2)}) collective-permute-start(f32[512,512]{1,0:T(8,128)S(1)} %convolution_select_fusion.1), channel_id=1, source_target_pairs={{64,0},{65,1},{66,2},{67,3},{68,4},{69,5},{70,6},{71,7},{72,8},{73... | collective-permute-start | bytes 3145736 | tf_op jit(solution)/shard_map/ppermute | solution.py:48
  403.7 19.1 %collective-permute-start.24 = (f32[4,512]{1,0:T(4,128)S(1)}, f32[4,512]{1,0:T(4,128)S(1)}, u32[]{:S(2)}, u32[]{:S(2)}) collective-permute-start(f32[4,512]{1,0:T(4,128)S(1)} %fusion.22), channel_id=1, source_target_pairs={{8,0},{9,1},{10,2},{11,3},{12,4},{13,5},{14,6},{15,7},{16,8},{17,9... | collective-permute-start | bytes 24584 | tf_op jit(solution)/shard_map/ppermute | solution.py:48
  425.0 8.6 %collective-permute-start.26 = (f32[4,512]{1,0:T(4,128)S(1)}, f32[4,512]{1,0:T(4,128)S(1)}, u32[]{:S(2)}, u32[]{:S(2)}) collective-permute-start(f32[4,512]{1,0:T(4,128)S(1)} %fusion.21), channel_id=1, source_target_pairs={{16,0},{17,1},{18,2},{19,3},{20,4},{21,5},{22,6},{23,7},{24,8},{25... | collective-permute-start | bytes 24584 | tf_op jit(solution)/shard_map/ppermute | solution.py:48
  435.7 10.4 %collective-permute-start.28 = (f32[4,512]{1,0:T(4,128)S(1)}, f32[4,512]{1,0:T(4,128)S(1)}, u32[]{:S(2)}, u32[]{:S(2)}) collective-permute-start(f32[4,512]{1,0:T(4,128)S(1)} %fusion.20), channel_id=1, source_target_pairs={{32,0},{33,1},{34,2},{35,3},{36,4},{37,5},{38,6},{39,7},{40,8},{41... | collective-permute-start | bytes 24584 | tf_op jit(solution)/shard_map/ppermute | solution.py:48
  454.8 7.1 %collective-permute-start.32 = (f32[4,512]{1,0:T(4,128)S(1)}, f32[4,512]{1,0:T(4,128)S(1)}, u32[]{:S(2)}, u32[]{:S(2)}) collective-permute-start(f32[4,512]{1,0:T(4,128)S(1)} %fusion.18), channel_id=1, source_target_pairs={{128,0},{129,1},{130,2},{131,3},{132,4},{133,5},{134,6},{135,7},{1... | collective-permute-start | bytes 24584 | tf_op jit(solution)/shard_map/ppermute | solution.py:48
  (14 other events, 434.9 us)
